TPU v7x, 32 devices: a whole 2x2x4 slice. The times are simulated.
32 devices in a mesh: ctx: 16 (over z, x, core), head: 2 (over y).
Axes of the slice: x: 2, y: 2, z: 4, core: 2. Of those that a mesh axis runs over, the one named last changes fastest.
Arguments:
- attn_q: bfloat16 [4096, 8192], P(('ctx', 'head')), may hold values from -8 to 8
- attn_k: bfloat16 [4096, 8192], P(('ctx', 'head')), may hold values from -8 to 8
- attn_v: bfloat16 [4096, 8192], P(('ctx', 'head')), may hold values from -5 to 5
- attn_dout: bfloat16 [4096, 8192], P(('ctx', 'head')), may hold values from -5 to 5
- doc_ids: int32 [4096], replicated, may hold values from 0 to 7, never falling along the last dimension, each value on 1 to 1024 neighbouring positions
Outputs:
- attn_dq: bfloat16 [4096, 8192], P('ctx', 'head')
- attn_dk: bfloat16 [4096, 8192], P('ctx', 'head')
- attn_dv: bfloat16 [4096, 8192], P('ctx', 'head')
Inputs may be any that keep to these rules, and one draw needn't show every extreme that they name: `doc_ids`: document numbers never fall along the window; each document holds 1 to 1024 consecutive tokens, and one holds exactly 1024.
All inputs are finite; a program needn't handle non-finite values.
Results may differ from a plain program's by a relative error of at most 0.0088.
Values may be sent and summed in bfloat16 or wider, within the bound.
No kernel may reach another device: no remote copies, remote signals or barrier semaphores. Data moves between devices by JAX's collectives and lax.ppermute only.
A program may use at most 256 MiB of HBM per device.

v0:
```python
from functools import reduce
import jax
import jax.numpy as jnp
from jax import lax
from jax.sharding import PartitionSpec as P

HEAD_DIM = 128
REACH = 4
masked_value = -1e30


def shifted(value, axis, steps):
    count = lax.axis_size(axis)
    leading, last = (max(0, -steps), min(count, count - steps))
    return lax.ppermute(value, axis, [(source, source + steps) for source in range(leading, last)])


def per_device(attn_q, attn_k, attn_v, attn_dout, doc_ids):
    query, keys, values, dout = (
        lax.all_to_all(attn_q, "head", split_axis=1, concat_axis=0, tiled=True),
        lax.all_to_all(attn_k, "head", split_axis=1, concat_axis=0, tiled=True),
        lax.all_to_all(attn_v, "head", split_axis=1, concat_axis=0, tiled=True),
        lax.all_to_all(attn_dout, "head", split_axis=1, concat_axis=0, tiled=True),
    )
    tok = query.shape[0]
    width = query.shape[1]
    heads_local = width // HEAD_DIM
    ctx_count = lax.axis_size("ctx")
    ctx_pos = lax.axis_index("ctx")
    scale = HEAD_DIM ** (-0.5)

    def head_major(block):
        return jnp.transpose(block.reshape(tok, heads_local, HEAD_DIM), (1, 0, 2))

    q_own = head_major(query)
    k_own = head_major(keys)
    v_own = head_major(values)
    d_own = head_major(dout)
    row_ids = jnp.arange(tok, dtype=jnp.int32)

    def block_info(owner):
        start = jnp.clip(owner * tok, 0, tok * (ctx_count - 1))
        docs = lax.dynamic_slice_in_dim(doc_ids, start, tok)
        return (owner * tok + row_ids, docs, (owner >= 0) & (owner < ctx_count))

    def allowed(q_info, k_info):
        causal = k_info[0][None, :] <= q_info[0][:, None]
        same_doc = k_info[1][None, :] == q_info[1][:, None]
        return causal & same_doc & q_info[2] & k_info[2]

    def scores(q_blk, k_blk, mask):
        raw = jnp.einsum("hqd,hkd->hqk", q_blk, k_blk, preferred_element_type=jnp.float32) * scale
        return jnp.where(mask[None], raw, masked_value)

    own = block_info(ctx_pos)
    key_list = [k_own]
    value_list = [v_own]
    masks = [allowed(own, own)]
    for shift in range(1, REACH + 1):
        far_k, far_v = shifted((k_own, v_own), "ctx", shift)
        key_list.append(far_k)
        value_list.append(far_v)
        masks.append(allowed(own, block_info(ctx_pos - shift)))
    logits = [scores(q_own, key_list[index], masks[index]) for index in range(REACH + 1)]
    top = reduce(jnp.maximum, [jnp.max(item, axis=2) for item in logits])
    denom = reduce(jnp.add, [jnp.sum(jnp.exp(item - top[:, :, None]), axis=2) for item in logits])
    lse = top + jnp.log(denom)
    probs = [
        jnp.where(masks[index][None], jnp.exp(logits[index] - lse[:, :, None]), 0.0)
        for index in range(REACH + 1)
    ]
    attn_out = reduce(
        jnp.add,
        [
            jnp.einsum(
                "hqk,hkd->hqd",
                probs[index].astype(jnp.bfloat16),
                value_list[index],
                preferred_element_type=jnp.float32,
            )
            for index in range(REACH + 1)
        ],
    )
    delta = jnp.sum(d_own.astype(jnp.float32) * attn_out, axis=2)
    shape3 = (heads_local, tok, HEAD_DIM)
    dq_acc = jnp.zeros(shape3, jnp.float32)
    dk_acc = jnp.zeros(shape3, jnp.float32)
    dv_acc = jnp.zeros(shape3, jnp.float32)
    for index in range(REACH + 1):
        k_blk = key_list[index]
        v_blk = value_list[index]
        prob = probs[index]
        prob_bf = prob.astype(jnp.bfloat16)
        dprobs = jnp.einsum("hqd,hkd->hqk", d_own, v_blk, preferred_element_type=jnp.float32)
        dscores = (prob * (dprobs - delta[:, :, None])).astype(jnp.bfloat16)
        dq_acc = dq_acc + jnp.einsum(
            "hqk,hkd->hqd", dscores, k_blk, preferred_element_type=jnp.float32
        )
        if index == 0:
            dk_acc = (
                jnp.einsum("hqk,hqd->hkd", dscores, q_own, preferred_element_type=jnp.float32)
                * scale
            )
            dv_acc = jnp.einsum("hqk,hqd->hkd", prob_bf, d_own, preferred_element_type=jnp.float32)
    for shift in range(1, REACH + 1):
        q_blk, d_blk = shifted((q_own, d_own), "ctx", -shift)
        far_lse, far_delta = shifted((lse, delta), "ctx", -shift)
        mask = allowed(block_info(ctx_pos + shift), own)
        logit = scores(q_blk, k_own, mask)
        prob = jnp.where(mask[None], jnp.exp(logit - far_lse[:, :, None]), 0.0)
        prob_bf = prob.astype(jnp.bfloat16)
        dprobs = jnp.einsum("hqd,hkd->hqk", d_blk, v_own, preferred_element_type=jnp.float32)
        dscores = (prob * (dprobs - far_delta[:, :, None])).astype(jnp.bfloat16)
        dk_acc = (
            dk_acc
            + jnp.einsum("hqk,hqd->hkd", dscores, q_blk, preferred_element_type=jnp.float32) * scale
        )
        dv_acc = dv_acc + jnp.einsum(
            "hqk,hqd->hkd", prob_bf, d_blk, preferred_element_type=jnp.float32
        )

    def token_major(block):
        return jnp.transpose(block, (1, 0, 2)).reshape(tok, width)

    attn_dq = token_major((dq_acc * scale).astype(jnp.bfloat16))
    attn_dk = token_major(dk_acc.astype(jnp.bfloat16))
    attn_dv = token_major(dv_acc.astype(jnp.bfloat16))
    return (attn_dq, attn_dk, attn_dv)


def solution(mesh):
    return jax.shard_map(
        per_device,
        mesh=mesh,
        in_specs=(
            P(("ctx", "head"), None),
            P(("ctx", "head"), None),
            P(("ctx", "head"), None),
            P(("ctx", "head"), None),
            P(),
        ),
        out_specs=(P("ctx", "head"), P("ctx", "head"), P("ctx", "head")),
        check_vma=False,
    )
```

profile of v0, /device:TPU:31, one launch (start us, length us, event | category | flops | bytes accessed | tf_op | source)
XLA Modules:
  0.0 671.9 jit_solution(12698922298471909461)
XLA Ops:
  0.6 3.1 copy.248
  3.8 4.0 all-to-all-start.1
  7.7 3.1 copy.249
  10.9 20.0 %all-to-all-done.1 = bf16[128,2,4096]{2,0,1:T(8,128)(2,1)S(1)} async-done(((bf16[128,2,4096]{2,0,1:T(8,128)(2,1)}), bf16[128,2,4096]{2,0,1:T(8,128)(2,1)S(1)}, u32[]{:S(2)}, u32[]{:S(2)}) %all-to-all-start.1) | async-done | bytes 2097184 | tf_op jit(solution)/shard_map/all_to_all | solution.py:21
  32.2 4.9 all-to-all-start
  37.1 3.1 copy.246
  40.2 19.0 %all-to-all-done = bf16[128,2,4096]{2,0,1:T(8,128)(2,1)S(1)} async-done(((bf16[128,2,4096]{2,0,1:T(8,128)(2,1)}), bf16[128,2,4096]{2,0,1:T(8,128)(2,1)S(1)}, u32[]{:S(2)}, u32[]{:S(2)}) %all-to-all-start) | async-done | bytes 2097184 | tf_op jit(solution)/shard_map/all_to_all | solution.py:20
  59.2 6.0 all-to-all-start.3
  65.2 2.2 copy.185
  72.3 14.2 %all-to-all-done.3 = bf16[128,2,4096]{2,0,1:T(8,128)(2,1)} async-done(((bf16[128,2,4096]{2,0,1:T(8,128)(2,1)}), bf16[128,2,4096]{2,0,1:T(8,128)(2,1)}, u32[]{:S(2)}, u32[]{:S(2)}) %all-to-all-start.3) | async-done | bytes 2097184 | tf_op jit(solution)/shard_map/all_to_all | solution.py:22
  86.5 6.0 all-to-all-start.2
  98.0 3.4 copy.184
  108.3 4.6 all-to-all-done.2
  112.9 2.2 copy.186
  115.1 2.2 copy.253
  119.5 6.0 fusion.9
  127.0 3.9 fusion.12
  130.9 36.1 %collective-permute-done.3 = bf16[32,256,128]{2,1,0:T(8,128)(2,1)} collective-permute-done((bf16[32,256,128]{2,1,0:T(8,128)(2,1)}, bf16[32,256,128]{2,1,0:T(8,128)(2,1)}, u32[]{:S(2)}, u32[]{:S(2)}) %collective-permute-start.3) | collective-permute-done | bytes 2097184 | tf_op jit(solution)/shard_map/ppermute | solution.py:15
  168.3 3.9 fusion.13
  173.5 5.5 fusion.11
  179.0 82.5 %collective-permute-start.16 = (bf16[32,256,128]{2,1,0:T(8,128)(2,1)}, bf16[32,256,128]{2,1,0:T(8,128)(2,1)}, u32[]{:S(2)}, u32[]{:S(2)}) collective-permute-start(bf16[32,256,128]{2,1,0:T(8,128)(2,1)} %bitcast.136), channel_id=1, source_target_pairs={{6,0},{8,2},{10,4},{12,6},{14,8},{16,10},{18,12},{20,14},{22,16},{... | collective-permute-start | bytes 6291464 | tf_op jit(solution)/shard_map/ppermute | solution.py:15
  261.6 7.2 %fusion.10 = (f32[32,256]{1,0:T(8,128)S(1)}, f32[32,256,256]{1,2,0:T(8,128)}) fusion(pred[256,256]{0,1:T(8,128)(4,1)S(1)} %get-tuple-element.25, bf16[32,256,128]{2,1,0:T(8,128)(2,1)} %collective-permute-done, bf16[256,32,128]{2,1,0:T(8,128)(2,1)S(1)} %bitcast.149), kind=kOutput, calls=%fused_computation.38 | convolution fusion | flops 543154176 | bytes 12681216 | tf_op jit(solution)/shard_map/hqd,hkd->hqk/dot_general | solution.py:52
  268.8 12.7 %exponential_reduce_fusion.3 = (f32[32,256]{1,0:T(8,128)S(1)}, f32[32,256]{1,0:T(8,128)S(1)}, f32[32,256]{1,0:T(8,128)S(1)}, f32[32,256]{1,0:T(8,128)S(1)}, f32[32,256]{1,0:T(8,128)S(1)}) fusion(f32[32,256,256]{1,2,0:T(8,128)} %get-tuple-element.41, f32[32,256]{1,0:T(8,128)S(1)} %maximum_maximum_fusion, pred[256,256]{0,1:T(8,128)(4,1)S(1)} %get-tuple-element.25, ...), kind=kLoop, calls=%fused_computation.21 | loop fusion | flops 41902080 | bytes 42467328 | tf_op jit(solution)/shard_map/reduce_sum | solution.py:66
  281.5 3.0 collective-permute-start.12
  284.6 6.2 fusion.24
  290.8 25.0 %collective-permute-start.18 = (bf16[32,256,128]{2,1,0:T(8,128)(2,1)}, bf16[32,256,128]{2,1,0:T(8,128)(2,1)}, u32[]{:S(2)}, u32[]{:S(2)}) collective-permute-start(bf16[32,256,128]{2,1,0:T(8,128)(2,1)} %bitcast.134), channel_id=1, source_target_pairs={{6,0},{8,2},{10,4},{12,6},{14,8},{16,10},{18,12},{20,14},{22,16},{... | collective-permute-start | bytes 6291464 | tf_op jit(solution)/shard_map/ppermute | solution.py:15
  315.8 4.6 fusion.26
  320.4 37.2 %collective-permute-start.14 = (bf16[32,256,128]{2,1,0:T(8,128)(2,1)}, bf16[32,256,128]{2,1,0:T(8,128)(2,1)}, u32[]{:S(2)}, u32[]{:S(2)}) collective-permute-start(bf16[32,256,128]{2,1,0:T(8,128)(2,1)} %bitcast.134), channel_id=1, source_target_pairs={{4,0},{6,2},{8,4},{10,6},{12,8},{14,10},{16,12},{18,14},{20,16},{2... | collective-permute-start | bytes 6291464 | tf_op jit(solution)/shard_map/ppermute | solution.py:15
  357.6 6.2 fusion.28
  363.9 9.1 %fusion.108 = f32[32,256,128]{2,1,0:T(8,128)} fusion(bf16[32,256,128]{2,0,1:T(8,128)(2,1)S(1)} %bitcast.163, f32[32,256,256]{1,2,0:T(8,128)} %get-tuple-element.39, f32[32,256]{1,0:T(8,128)S(1)} %log_add_fusion, pred[256,256]{0,1:T(8,128)(4,1)S(1)} %get-tuple-element.24), kind=kOutput, calls=%fused_computation.128 | convolution fusion | flops 547356672 | bytes 14778368 | tf_op jit(solution)/shard_map/hqk,hkd->hqd/dot_general | solution.py:75
  372.9 17.5 %collective-permute-done.7 = bf16[32,256,128]{2,1,0:T(8,128)(2,1)} collective-permute-done((bf16[32,256,128]{2,1,0:T(8,128)(2,1)}, bf16[32,256,128]{2,1,0:T(8,128)(2,1)}, u32[]{:S(2)}, u32[]{:S(2)}) %collective-permute-start.7) | collective-permute-done | bytes 2097184 | tf_op jit(solution)/shard_map/ppermute | solution.py:15
  390.4 2.8 collective-permute-start.8
  393.3 14.4 %multiply_reduce_fusion = f32[32,256]{1,0:T(8,128)S(1)} fusion(f32[32,256,128]{2,1,0:T(8,128)} %fusion.24, f32[32,256,128]{2,1,0:T(8,128)} %fusion.26, f32[32,256,128]{2,1,0:T(8,128)} %fusion.108, f32[32,256,128]{2,1,0:T(8,128)} %fusion.28, bf16[32,256,128]{2,1,0:T(8,128)(2,1)} %collective-permute-done.7, f32[32,256,256]{1,2,0:T(8,128)} %copy-done, ...), kind=kOutput, calls=%fused_computation.57 | convolution fusion | flops 554688512 | bytes 29491200 | tf_op jit(solution)/shard_map/hqk,hkd->hqd/dot_general | solution.py:75
  407.7 10.3 %multiply_convert_fusion.8 = bf16[32,256,256]{1,2,0:T(8,128)(2,1)} fusion(f32[32,256,256]{1,2,0:T(8,128)} %get-tuple-element.39, f32[32,256]{1,0:T(8,128)S(1)} %multiply_reduce_fusion, f32[32,256]{1,0:T(8,128)S(1)} %log_add_fusion, pred[256,256]{0,1:T(8,128)(4,1)S(1)} %get-tuple-element.24, bf16[256,32,128]{2,1,0:T(8,128)(2,1)} %bitcast.162, ...), kind=kOutput, calls=%fused_computation.12 | convolution fusion | flops 551550976 | bytes 16908288 | tf_op jit(solution)/shard_map/hqd,hkd->hqk/dot_general | solution.py:94
  418.0 11.7 %fusion.64 = f32[32,256,128]{1,2,0:T(8,128)} fusion(bf16[32,256,128]{2,1,0:T(8,128)(2,1)} %collective-permute-done.2, f32[32,256,256]{1,2,0:T(8,128)} %copy-done.5, f32[32,256]{1,0:T(8,128)S(1)} %multiply_reduce_fusion, f32[32,256]{1,0:T(8,128)S(1)} %log_add_fusion, pred[256,256]{0,1:T(8,128)(4,1)S(1)} %get-tuple-element.27, ...), kind=kOutput, calls=%fused_computation.88 | convolution fusion | flops 1088421888 | bytes 19005440 | tf_op jit(solution)/shard_map/hqk,hkd->hqd/dot_general | solution.py:96
  429.7 11.5 %fusion.63 = f32[32,256,128]{1,2,0:T(8,128)} fusion(bf16[32,256,128]{2,1,0:T(8,128)(2,1)} %collective-permute-done.1, f32[32,256,256]{1,2,0:T(8,128)} %copy-done.6, f32[32,256]{1,0:T(8,128)S(1)} %multiply_reduce_fusion, f32[32,256]{1,0:T(8,128)S(1)} %log_add_fusion, pred[256,256]{0,1:T(8,128)(4,1)S(1)} %get-tuple-element.26, ...), kind=kOutput, calls=%fused_computation.87 | convolution fusion | flops 1088421888 | bytes 19005440 | tf_op jit(solution)/shard_map/hqk,hkd->hqd/dot_general | solution.py:96
  441.2 11.4 %fusion.62 = f32[32,256,128]{1,2,0:T(8,128)} fusion(bf16[32,256,128]{2,1,0:T(8,128)(2,1)} %collective-permute-done, f32[32,256,256]{1,2,0:T(8,128)} %get-tuple-element.41, f32[32,256]{1,0:T(8,128)S(1)} %multiply_reduce_fusion, f32[32,256]{1,0:T(8,128)S(1)} %log_add_fusion, pred[256,256]{0,1:T(8,128)(4,1)S(1)} %get-tuple-element.25, ...), kind=kOutput, calls=%fused_computation.86 | convolution fusion | flops 1088421888 | bytes 19005440 | tf_op jit(solution)/shard_map/hqk,hkd->hqd/dot_general | solution.py:96
  452.7 5.8 fusion.106
  458.4 14.7 %multiply_convert_fusion.10 = bf16[32,256,128]{1,2,0:T(8,128)(2,1)} fusion(f32[32,256,128]{1,2,0:T(8,128)} %fusion.64, f32[32,256,128]{1,2,0:T(8,128)} %fusion.63, f32[32,256,128]{1,2,0:T(8,128)} %fusion.106, f32[32,256,128]{1,2,0:T(8,128)} %fusion.62, bf16[32,256,128]{2,1,0:T(8,128)(2,1)} %collective-permute-done.3, f32[32,256,256]{1,2,0:T(8,128)} %copy-done, ...), kind=kOutput, calls=%fused_computation.51 | convolution fusion | flops 1094713344 | bytes 33685504 | tf_op jit(solution)/shard_map/hqk,hkd->hqd/dot_general | solution.py:96
  474.9 6.1 fusion.169
  481.0 2.6 collective-permute-start.10
  483.6 6.3 fusion.170
  489.8 2.8 collective-permute-start.19
  492.7 6.1 fusion.171
  498.8 5.3 fusion.102
  504.2 14.1 %collective-permute-done.20 = bf16[32,256,128]{2,1,0:T(8,128)(2,1)S(1)} collective-permute-done((bf16[32,256,128]{2,1,0:T(8,128)(2,1)}, bf16[32,256,128]{2,1,0:T(8,128)(2,1)S(1)}, u32[]{:S(2)}, u32[]{:S(2)}) %collective-permute-start.20) | collective-permute-done | bytes 2097184 | tf_op jit(solution)/shard_map/ppermute | solution.py:15
  519.6 4.6 fusion.172
  524.2 3.7 fusion.104
  527.8 4.2 copy.119
  532.1 5.7 collective-permute-start.22
  539.2 2.4 collective-permute-start.13
  541.6 10.9 %fusion.68 = f32[32,256,128]{1,2,0:T(8,128)} fusion(bf16[32,256,128]{2,1,0:T(8,128)(2,1)} %collective-permute-done.16, f32[32,256,256]{1,2,0:T(8,128)} %fusion.169, f32[32,256]{1,0:T(8,128)S(1)} %collective-permute-done.19, f32[32,256]{1,0:T(8,128)S(1)} %collective-permute-done.17, pred[256,256]{0,1:T(8,128)(4,1)S(1)} %get-tuple-element.31, ...), kind=kOutput, calls=%fused_computation.92 | convolution fusion | flops 1088421888 | bytes 19005440 | tf_op jit(solution)/shard_map/hqk,hqd->hkd/dot_general | solution.py:116
  552.5 10.3 %collective-permute-start.11 = (f32[32,256]{1,0:T(8,128)S(1)}, f32[32,256]{1,0:T(8,128)S(1)}, u32[]{:S(2)}, u32[]{:S(2)}) collective-permute-start(f32[32,256]{1,0:T(8,128)S(1)} %multiply_reduce_fusion), channel_id=1, source_target_pairs={{2,0},{4,2},{6,4},{8,6},{10,8},{12,10},{14,12},{16,14},{18,16},{20... | collective-permute-start | bytes 98312 | tf_op jit(solution)/shard_map/ppermute | solution.py:15
  562.9 4.7 collective-permute-start.9
  567.6 25.2 %collective-permute-start.23 = (f32[32,256]{1,0:T(8,128)S(1)}, f32[32,256]{1,0:T(8,128)S(1)}, u32[]{:S(2)}, u32[]{:S(2)}) collective-permute-start(f32[32,256]{1,0:T(8,128)S(1)} %multiply_reduce_fusion), channel_id=1, source_target_pairs={{8,0},{10,2},{12,4},{14,6},{16,8},{18,10},{20,12},{22,14},{24,16},... | collective-permute-start | bytes 98312 | tf_op jit(solution)/shard_map/ppermute | solution.py:15
  592.8 10.9 %fusion.67 = f32[32,256,128]{1,2,0:T(8,128)} fusion(bf16[32,256,128]{2,1,0:T(8,128)(2,1)} %collective-permute-done.12, f32[32,256,256]{1,2,0:T(8,128)} %fusion.170, f32[32,256]{1,0:T(8,128)S(1)} %collective-permute-done.15, f32[32,256]{1,0:T(8,128)S(1)} %collective-permute-done.13, pred[256,256]{0,1:T(8,128)(4,1)S(1)} %get-tuple-element.30, ...), kind=kOutput, calls=%fused_computation.91 | convolution fusion | flops 1088421888 | bytes 19005440 | tf_op jit(solution)/shard_map/hqk,hqd->hkd/dot_general | solution.py:116
  605.9 11.0 %fusion.66 = f32[32,256,128]{1,2,0:T(8,128)} fusion(bf16[32,256,128]{2,1,0:T(8,128)(2,1)} %collective-permute-done.8, f32[32,256,256]{1,2,0:T(8,128)} %fusion.171, f32[32,256]{1,0:T(8,128)S(1)} %collective-permute-done.11, f32[32,256]{1,0:T(8,128)S(1)} %collective-permute-done.9, pred[256,256]{0,1:T(8,128)(4,1)S(1)} %get-tuple-element.29, ...), kind=kOutput, calls=%fused_computation.90 | convolution fusion | flops 1088421888 | bytes 19005440 | tf_op jit(solution)/shard_map/hqk,hqd->hkd/dot_general | solution.py:116
  616.9 13.0 %multiply_convert_fusion.9 = bf16[32,256,128]{1,2,0:T(8,128)(2,1)} fusion(f32[32,256,128]{1,2,0:T(8,128)} %fusion.68, f32[32,256,128]{1,2,0:T(8,128)} %fusion.67, f32[32,256,128]{1,2,0:T(8,128)} %fusion.104, f32[32,256,128]{1,2,0:T(8,128)} %fusion.66, bf16[32,256,128]{2,1,0:T(8,128)(2,1)} %copy-done.12, f32[32,256,256]{1,2,0:T(8,128)} %fusion.172, ...), kind=kOutput, calls=%fused_computation.50 | convolution fusion | flops 1094713344 | bytes 33685504 | tf_op jit(solution)/shard_map/hqk,hqd->hkd/dot_general | solution.py:116
  629.9 4.3 copy.120
  634.2 8.4 %fusion.16 = f32[32,256,128]{1,2,0:T(8,128)} fusion(bf16[32,256,128]{2,1,0:T(8,128)(2,1)} %collective-permute-done.18, f32[32,256,256]{1,2,0:T(8,128)} %fusion.169, f32[32,256]{1,0:T(8,128)S(1)} %collective-permute-done.17, pred[256,256]{0,1:T(8,128)(4,1)S(1)} %get-tuple-element.31), kind=kOutput, calls=%fused_computation.43 | convolution fusion | flops 547356672 | bytes 14778368 | tf_op jit(solution)/shard_map/hqk,hqd->hkd/dot_general | solution.py:118
  642.7 8.5 %fusion.18 = f32[32,256,128]{1,2,0:T(8,128)} fusion(bf16[32,256,128]{2,1,0:T(8,128)(2,1)} %collective-permute-done.14, f32[32,256,256]{1,2,0:T(8,128)} %fusion.170, f32[32,256]{1,0:T(8,128)S(1)} %collective-permute-done.13, pred[256,256]{0,1:T(8,128)(4,1)S(1)} %get-tuple-element.30), kind=kOutput, calls=%fused_computation.44 | convolution fusion | flops 547356672 | bytes 14778368 | tf_op jit(solution)/shard_map/hqk,hqd->hkd/dot_general | solution.py:118
  651.1 5.9 fusion.20
  657.1 11.5 %add_convert_fusion = bf16[32,256,128]{1,2,0:T(8,128)(2,1)S(1)} fusion(f32[32,256,128]{1,2,0:T(8,128)} %fusion.16, f32[32,256,128]{1,2,0:T(8,128)} %fusion.18, f32[32,256,128]{1,2,0:T(8,128)} %fusion.102, f32[32,256,128]{1,2,0:T(8,128)} %fusion.20, bf16[32,256,128]{2,1,0:T(8,128)(2,1)} %collective-permute-done.22, f32[32,256,256]{1,2,0:T(8,128)} %fusion.172, ...), kind=kOutput, calls=%fused_computation.52 | convolution fusion | flops 552599552 | bytes 29458432 | tf_op jit(solution)/shard_map/hqk,hqd->hkd/dot_general | solution.py:118
  668.6 2.9 copy.121
  (98 shorter events, 31.5 us)
Async XLA Ops:
  3.8 27.1 %all-to-all-start.1 = ((bf16[128,2,4096]{2,0,1:T(8,128)(2,1)}), bf16[128,2,4096]{2,0,1:T(8,128)(2,1)S(1)}, u32[]{:S(2)}, u32[]{:S(2)}) async-start(bf16[128,2,4096]{2,0,1:T(8,128)(2,1)} %bitcast.178), calls=%async_computation.1 | async-start | bytes 4194304 | tf_op jit(solution)/shard_map/all_to_all | solution.py:21
  30.8 1.3 copy-start.13
  32.2 27.0 %all-to-all-start = ((bf16[128,2,4096]{2,0,1:T(8,128)(2,1)}), bf16[128,2,4096]{2,0,1:T(8,128)(2,1)S(1)}, u32[]{:S(2)}, u32[]{:S(2)}) async-start(bf16[128,2,4096]{2,0,1:T(8,128)(2,1)} %bitcast.177), calls=%async_computation | async-start | bytes 4194304 | tf_op jit(solution)/shard_map/all_to_all | solution.py:20
  59.2 6.0 copy-start.11
  59.2 27.3 %all-to-all-start.3 = ((bf16[128,2,4096]{2,0,1:T(8,128)(2,1)}), bf16[128,2,4096]{2,0,1:T(8,128)(2,1)}, u32[]{:S(2)}, u32[]{:S(2)}) async-start(bf16[128,2,4096]{2,0,1:T(8,128)(2,1)} %bitcast.176), calls=%async_computation.3 | async-start | bytes 4194304 | tf_op jit(solution)/shard_map/all_to_all | solution.py:22
  65.2 5.6 copy-start.14
  69.5 55.9 %collective-permute-start.2 = (bf16[32,256,128]{2,1,0:T(8,128)(2,1)}, bf16[32,256,128]{2,1,0:T(8,128)(2,1)}, u32[]{:S(2)}, u32[]{:S(2)}) collective-permute-start(bf16[32,256,128]{2,1,0:T(8,128)(2,1)} %bitcast.135), channel_id=1, source_target_pairs={{0,6},{2,8},{4,10},{6,12},{8,14},{10,16},{12,18},{14,20},{16,22},{... | collective-permute-start | bytes 6291464 | tf_op jit(solution)/shard_map/ppermute | solution.py:15
  70.8 23.0 %copy-start.16 = (s32[4096]{0:T(1024)S(1)}, s32[4096]{0:T(1024)}, u32[]{:S(2)}) copy-start(s32[4096]{0:T(1024)} %param.9) | copy-start | bytes 49156
  86.5 26.4 %all-to-all-start.2 = ((bf16[128,2,4096]{2,0,1:T(8,128)(2,1)}), bf16[128,2,4096]{2,0,1:T(8,128)(2,1)}, u32[]{:S(2)}, u32[]{:S(2)}) async-start(bf16[128,2,4096]{2,0,1:T(8,128)(2,1)} %bitcast.174), calls=%async_computation.2 | async-start | bytes 4194304 | tf_op jit(solution)/shard_map/all_to_all | solution.py:23
  92.5 74.5 %collective-permute-start.3 = (bf16[32,256,128]{2,1,0:T(8,128)(2,1)}, bf16[32,256,128]{2,1,0:T(8,128)(2,1)}, u32[]{:S(2)}, u32[]{:S(2)}) collective-permute-start(bf16[32,256,128]{2,1,0:T(8,128)(2,1)} %bitcast.135), channel_id=1, source_target_pairs={{0,8},{2,10},{4,12},{6,14},{8,16},{10,18},{12,20},{14,22},{16,24},... | collective-permute-start | bytes 6291464 | tf_op jit(solution)/shard_map/ppermute | solution.py:15
  94.0 78.2 %collective-permute-start.1 = (bf16[32,256,128]{2,1,0:T(8,128)(2,1)}, bf16[32,256,128]{2,1,0:T(8,128)(2,1)}, u32[]{:S(2)}, u32[]{:S(2)}) collective-permute-start(bf16[32,256,128]{2,1,0:T(8,128)(2,1)} %bitcast.135), channel_id=1, source_target_pairs={{0,4},{2,6},{4,8},{6,10},{8,12},{10,14},{12,16},{14,18},{16,20},{1... | collective-permute-start | bytes 6291464 | tf_op jit(solution)/shard_map/ppermute | solution.py:15
  96.7 82.3 %collective-permute-start = (bf16[32,256,128]{2,1,0:T(8,128)(2,1)}, bf16[32,256,128]{2,1,0:T(8,128)(2,1)}, u32[]{:S(2)}, u32[]{:S(2)}) collective-permute-start(bf16[32,256,128]{2,1,0:T(8,128)(2,1)} %bitcast.135), channel_id=1, source_target_pairs={{0,2},{2,4},{4,6},{6,8},{8,10},{10,12},{12,14},{14,16},{16,18},{18... | collective-permute-start | bytes 6291464 | tf_op jit(solution)/shard_map/ppermute | solution.py:15
  103.5 1.4 copy-start.7
  107.0 174.5 %collective-permute-start.6 = (bf16[32,256,128]{2,1,0:T(8,128)(2,1)}, bf16[32,256,128]{2,1,0:T(8,128)(2,1)}, u32[]{:S(2)}, u32[]{:S(2)}) collective-permute-start(bf16[32,256,128]{2,1,0:T(8,128)(2,1)} %bitcast.133), channel_id=1, source_target_pairs={{0,6},{2,8},{4,10},{6,12},{8,14},{10,16},{12,18},{14,20},{16,22},{... | collective-permute-start | bytes 6291464 | tf_op jit(solution)/shard_map/ppermute | solution.py:15
  112.9 2.2 copy-start.1
  115.1 4.4 copy-start.3
  125.5 165.3 %collective-permute-start.5 = (bf16[32,256,128]{2,1,0:T(8,128)(2,1)}, bf16[32,256,128]{2,1,0:T(8,128)(2,1)S(1)}, u32[]{:S(2)}, u32[]{:S(2)}) collective-permute-start(bf16[32,256,128]{2,1,0:T(8,128)(2,1)} %bitcast.133), channel_id=1, source_target_pairs={{0,4},{2,6},{4,8},{6,10},{8,12},{10,14},{12,16},{14,18},{16,20},{1... | collective-permute-start | bytes 6291464 | tf_op jit(solution)/shard_map/ppermute | solution.py:15
  130.9 153.7 %copy-start.5 = (f32[32,256,256]{1,2,0:T(8,128)}, f32[32,256,256]{1,2,0:T(8,128)S(1)}, u32[]{:S(2)}) copy-start(f32[32,256,256]{1,2,0:T(8,128)S(1)} %get-tuple-element.35) | copy-start | bytes 25165828
  167.0 153.5 %collective-permute-start.4 = (bf16[32,256,128]{2,1,0:T(8,128)(2,1)}, bf16[32,256,128]{2,1,0:T(8,128)(2,1)}, u32[]{:S(2)}, u32[]{:S(2)}) collective-permute-start(bf16[32,256,128]{2,1,0:T(8,128)(2,1)} %bitcast.133), channel_id=1, source_target_pairs={{0,2},{2,4},{4,6},{6,8},{8,10},{10,12},{12,14},{14,16},{16,18},{18... | collective-permute-start | bytes 6291464 | tf_op jit(solution)/shard_map/ppermute | solution.py:15
  172.2 96.6 %copy-start = (f32[32,256,256]{1,2,0:T(8,128)}, f32[32,256,256]{1,2,0:T(8,128)S(1)}, u32[]{:S(2)}) copy-start(f32[32,256,256]{1,2,0:T(8,128)S(1)} %get-tuple-element.33) | copy-start | bytes 25165828
  172.2 218.2 %collective-permute-start.7 = (bf16[32,256,128]{2,1,0:T(8,128)(2,1)}, bf16[32,256,128]{2,1,0:T(8,128)(2,1)}, u32[]{:S(2)}, u32[]{:S(2)}) collective-permute-start(bf16[32,256,128]{2,1,0:T(8,128)(2,1)} %bitcast.133), channel_id=1, source_target_pairs={{0,8},{2,10},{4,12},{6,14},{8,16},{10,18},{12,20},{14,22},{16,24},... | collective-permute-start | bytes 6291464 | tf_op jit(solution)/shard_map/ppermute | solution.py:15
  179.0 136.8 %copy-start.6 = (f32[32,256,256]{1,2,0:T(8,128)}, f32[32,256,256]{1,2,0:T(8,128)S(1)}, u32[]{:S(2)}) copy-start(f32[32,256,256]{1,2,0:T(8,128)S(1)} %get-tuple-element.37) | copy-start | bytes 25165828
  179.0 294.1 %collective-permute-start.16 = (bf16[32,256,128]{2,1,0:T(8,128)(2,1)}, bf16[32,256,128]{2,1,0:T(8,128)(2,1)}, u32[]{:S(2)}, u32[]{:S(2)}) collective-permute-start(bf16[32,256,128]{2,1,0:T(8,128)(2,1)} %bitcast.136), channel_id=1, source_target_pairs={{6,0},{8,2},{10,4},{12,6},{14,8},{16,10},{18,12},{20,14},{22,16},{... | collective-permute-start | bytes 6291464 | tf_op jit(solution)/shard_map/ppermute | solution.py:15
  281.5 199.5 %collective-permute-start.12 = (bf16[32,256,128]{2,1,0:T(8,128)(2,1)}, bf16[32,256,128]{2,1,0:T(8,128)(2,1)}, u32[]{:S(2)}, u32[]{:S(2)}) collective-permute-start(bf16[32,256,128]{2,1,0:T(8,128)(2,1)} %bitcast.136), channel_id=1, source_target_pairs={{4,0},{6,2},{8,4},{10,6},{12,8},{14,10},{16,12},{18,14},{20,16},{2... | collective-permute-start | bytes 6291464 | tf_op jit(solution)/shard_map/ppermute | solution.py:15
  290.8 29.6 %copy-start.17 = (bf16[32,256,128]{2,1,0:T(8,128)(2,1)}, bf16[32,256,128]{2,1,0:T(8,128)(2,1)S(1)}, u32[]{:S(2)}) copy-start(bf16[32,256,128]{2,1,0:T(8,128)(2,1)S(1)} %collective-permute-done.5) | copy-start | bytes 6291460
  290.8 66.8 %slice-start = ((s8[8388608]{0:T(1024)(128)(4,1)}), s8[4194304]{0:T(1024)(128)(4,1)S(1)}, s32[]{:S(2)}) async-start(s8[8388608]{0:T(1024)(128)(4,1)} %bitcast.159), calls=%async_computation.4 | async-start | bytes 8388608
  290.8 66.8 %slice-start.1 = ((s8[8388608]{0:T(1024)(128)(4,1)}), s8[4194304]{0:T(1024)(128)(4,1)S(1)}, s32[]{:S(2)}) async-start(s8[8388608]{0:T(1024)(128)(4,1)} %bitcast.159), calls=%async_computation.5 | async-start | bytes 8388608
  290.8 241.2 %collective-permute-start.18 = (bf16[32,256,128]{2,1,0:T(8,128)(2,1)}, bf16[32,256,128]{2,1,0:T(8,128)(2,1)}, u32[]{:S(2)}, u32[]{:S(2)}) collective-permute-start(bf16[32,256,128]{2,1,0:T(8,128)(2,1)} %bitcast.134), channel_id=1, source_target_pairs={{6,0},{8,2},{10,4},{12,6},{14,8},{16,10},{18,12},{20,14},{22,16},{... | collective-permute-start | bytes 6291464 | tf_op jit(solution)/shard_map/ppermute | solution.py:15
  320.4 43.4 %copy-start.8 = (bf16[32,8,32,128]{3,2,1,0:T(8,128)(2,1)S(1)}, bf16[32,8,32,128]{3,2,1,0:T(8,128)(2,1)}, u32[]{:S(2)}) copy-start(bf16[32,8,32,128]{3,2,1,0:T(8,128)(2,1)} %copy-done.7) | copy-start | bytes 6291460
  320.4 232.1 %collective-permute-start.14 = (bf16[32,256,128]{2,1,0:T(8,128)(2,1)}, bf16[32,256,128]{2,1,0:T(8,128)(2,1)}, u32[]{:S(2)}, u32[]{:S(2)}) collective-permute-start(bf16[32,256,128]{2,1,0:T(8,128)(2,1)} %bitcast.134), channel_id=1, source_target_pairs={{4,0},{6,2},{8,4},{10,6},{12,8},{14,10},{16,12},{18,14},{20,16},{2... | collective-permute-start | bytes 6291464 | tf_op jit(solution)/shard_map/ppermute | solution.py:15
  390.4 99.4 %collective-permute-start.8 = (bf16[32,256,128]{2,1,0:T(8,128)(2,1)}, bf16[32,256,128]{2,1,0:T(8,128)(2,1)}, u32[]{:S(2)}, u32[]{:S(2)}) collective-permute-start(bf16[32,256,128]{2,1,0:T(8,128)(2,1)} %bitcast.136), channel_id=1, source_target_pairs={{2,0},{4,2},{6,4},{8,6},{10,8},{12,10},{14,12},{16,14},{18,16},{20... | collective-permute-start | bytes 6291464 | tf_op jit(solution)/shard_map/ppermute | solution.py:15
  473.1 45.2 %collective-permute-start.20 = (bf16[32,256,128]{2,1,0:T(8,128)(2,1)}, bf16[32,256,128]{2,1,0:T(8,128)(2,1)S(1)}, u32[]{:S(2)}, u32[]{:S(2)}) collective-permute-start(bf16[32,256,128]{2,1,0:T(8,128)(2,1)} %bitcast.136), channel_id=1, source_target_pairs={{8,0},{10,2},{12,4},{14,6},{16,8},{18,10},{20,12},{22,14},{24,16},... | collective-permute-start | bytes 6291464 | tf_op jit(solution)/shard_map/ppermute | solution.py:15
  481.0 122.8 %collective-permute-start.10 = (bf16[32,256,128]{2,1,0:T(8,128)(2,1)}, bf16[32,256,128]{2,1,0:T(8,128)(2,1)}, u32[]{:S(2)}, u32[]{:S(2)}) collective-permute-start(bf16[32,256,128]{2,1,0:T(8,128)(2,1)} %bitcast.134), channel_id=1, source_target_pairs={{2,0},{4,2},{6,4},{8,6},{10,8},{12,10},{14,12},{16,14},{18,16},{20... | collective-permute-start | bytes 6291464 | tf_op jit(solution)/shard_map/ppermute | solution.py:15
  483.6 15.3 %slice-start.4 = ((s8[8388608]{0:T(1024)(128)(4,1)}), s8[4194304]{0:T(1024)(128)(4,1)S(1)}, s32[]{:S(2)}) async-start(s8[8388608]{0:T(1024)(128)(4,1)} %bitcast.179), calls=%async_computation.8 | async-start | bytes 8388608
  489.8 9.0 %copy-start.4 = (bf16[32,8,32,128]{3,2,1,0:T(8,128)(2,1)S(1)}, bf16[32,8,32,128]{3,2,1,0:T(8,128)(2,1)}, u32[]{:S(2)}) copy-start(bf16[32,8,32,128]{3,2,1,0:T(8,128)(2,1)} %copy-done.3) | copy-start | bytes 6291460
  489.8 9.0 %slice-start.5 = ((s8[8388608]{0:T(1024)(128)(4,1)}), s8[4194304]{0:T(1024)(128)(4,1)S(1)}, s32[]{:S(2)}) async-start(s8[8388608]{0:T(1024)(128)(4,1)} %bitcast.179), calls=%async_computation.9 | async-start | bytes 8388608
  489.8 47.9 %collective-permute-start.19 = (f32[32,256]{1,0:T(8,128)S(1)}, f32[32,256]{1,0:T(8,128)S(1)}, u32[]{:S(2)}, u32[]{:S(2)}) collective-permute-start(f32[32,256]{1,0:T(8,128)S(1)} %multiply_reduce_fusion), channel_id=1, source_target_pairs={{6,0},{8,2},{10,4},{12,6},{14,8},{16,10},{18,12},{20,14},{22,16},{... | collective-permute-start | bytes 98312 | tf_op jit(solution)/shard_map/ppermute | solution.py:15
  504.2 20.0 %copy-start.2 = (bf16[32,8,32,128]{3,2,1,0:T(8,128)(2,1)S(1)}, bf16[32,8,32,128]{3,2,1,0:T(8,128)(2,1)}, u32[]{:S(2)}) copy-start(bf16[32,8,32,128]{3,2,1,0:T(8,128)(2,1)} %copy.184) | copy-start | bytes 6291460
  504.2 20.0 %copy-start.10 = (bf16[32,256,256]{1,2,0:T(8,128)(2,1)S(1)}, bf16[32,256,256]{1,2,0:T(8,128)(2,1)}, u32[]{:S(2)}) copy-start(bf16[32,256,256]{1,2,0:T(8,128)(2,1)} %multiply_convert_fusion.8) | copy-start | bytes 12582916
  518.3 5.9 copy-start.12
  518.3 20.9 %collective-permute-start.17 = (f32[32,256]{1,0:T(8,128)S(1)}, f32[32,256]{1,0:T(8,128)S(1)}, u32[]{:S(2)}, u32[]{:S(2)}) collective-permute-start(f32[32,256]{1,0:T(8,128)S(1)} %log_add_fusion), channel_id=1, source_target_pairs={{6,0},{8,2},{10,4},{12,6},{14,8},{16,10},{18,12},{20,14},{22,16},{... | collective-permute-start | bytes 98312 | tf_op jit(solution)/shard_map/ppermute | solution.py:15
  527.8 13.8 %copy-start.9 = (bf16[32,8,32,128]{3,2,1,0:T(8,128)(2,1)S(1)}, bf16[32,8,32,128]{3,2,1,0:T(8,128)(2,1)}, u32[]{:S(2)}) copy-start(bf16[32,8,32,128]{3,2,1,0:T(8,128)(2,1)} %copy-done.7) | copy-start | bytes 6291460
  532.1 84.9 %collective-permute-start.22 = (bf16[32,256,128]{2,1,0:T(8,128)(2,1)}, bf16[32,256,128]{2,1,0:T(8,128)(2,1)}, u32[]{:S(2)}, u32[]{:S(2)}) collective-permute-start(bf16[32,256,128]{2,1,0:T(8,128)(2,1)} %bitcast.134), channel_id=1, source_target_pairs={{8,0},{10,2},{12,4},{14,6},{16,8},{18,10},{20,12},{22,14},{24,16},... | collective-permute-start | bytes 6291464 | tf_op jit(solution)/shard_map/ppermute | solution.py:15
  537.8 25.1 %collective-permute-start.15 = (f32[32,256]{1,0:T(8,128)S(1)}, f32[32,256]{1,0:T(8,128)S(1)}, u32[]{:S(2)}, u32[]{:S(2)}) collective-permute-start(f32[32,256]{1,0:T(8,128)S(1)} %multiply_reduce_fusion), channel_id=1, source_target_pairs={{4,0},{6,2},{8,4},{10,6},{12,8},{14,10},{16,12},{18,14},{20,16},{2... | collective-permute-start | bytes 98312 | tf_op jit(solution)/shard_map/ppermute | solution.py:15
  539.2 28.4 %collective-permute-start.13 = (f32[32,256]{1,0:T(8,128)S(1)}, f32[32,256]{1,0:T(8,128)S(1)}, u32[]{:S(2)}, u32[]{:S(2)}) collective-permute-start(f32[32,256]{1,0:T(8,128)S(1)} %log_add_fusion), channel_id=1, source_target_pairs={{4,0},{6,2},{8,4},{10,6},{12,8},{14,10},{16,12},{18,14},{20,16},{2... | collective-permute-start | bytes 98312 | tf_op jit(solution)/shard_map/ppermute | solution.py:15
  552.5 53.4 %collective-permute-start.11 = (f32[32,256]{1,0:T(8,128)S(1)}, f32[32,256]{1,0:T(8,128)S(1)}, u32[]{:S(2)}, u32[]{:S(2)}) collective-permute-start(f32[32,256]{1,0:T(8,128)S(1)} %multiply_reduce_fusion), channel_id=1, source_target_pairs={{2,0},{4,2},{6,4},{8,6},{10,8},{12,10},{14,12},{16,14},{18,16},{20... | collective-permute-start | bytes 98312 | tf_op jit(solution)/shard_map/ppermute | solution.py:15
  562.9 43.0 %collective-permute-start.9 = (f32[32,256]{1,0:T(8,128)S(1)}, f32[32,256]{1,0:T(8,128)S(1)}, u32[]{:S(2)}, u32[]{:S(2)}) collective-permute-start(f32[32,256]{1,0:T(8,128)S(1)} %log_add_fusion), channel_id=1, source_target_pairs={{2,0},{4,2},{6,4},{8,6},{10,8},{12,10},{14,12},{16,14},{18,16},{20... | collective-permute-start | bytes 98312 | tf_op jit(solution)/shard_map/ppermute | solution.py:15
  567.6 49.3 %collective-permute-start.23 = (f32[32,256]{1,0:T(8,128)S(1)}, f32[32,256]{1,0:T(8,128)S(1)}, u32[]{:S(2)}, u32[]{:S(2)}) collective-permute-start(f32[32,256]{1,0:T(8,128)S(1)} %multiply_reduce_fusion), channel_id=1, source_target_pairs={{8,0},{10,2},{12,4},{14,6},{16,8},{18,10},{20,12},{22,14},{24,16},... | collective-permute-start | bytes 98312 | tf_op jit(solution)/shard_map/ppermute | solution.py:15
  603.7 13.2 %collective-permute-start.21 = (f32[32,256]{1,0:T(8,128)S(1)}, f32[32,256]{1,0:T(8,128)S(1)}, u32[]{:S(2)}, u32[]{:S(2)}) collective-permute-start(f32[32,256]{1,0:T(8,128)S(1)} %log_add_fusion), channel_id=1, source_target_pairs={{8,0},{10,2},{12,4},{14,6},{16,8},{18,10},{20,12},{22,14},{24,16},... | collective-permute-start | bytes 98312 | tf_op jit(solution)/shard_map/ppermute | solution.py:15
  605.9 11.0 %copy-start.15 = (pred[256,256]{0,1:T(8,128)(4,1)S(1)}, pred[256,256]{0,1:T(8,128)(4,1)}, u32[]{:S(2)}) copy-start(pred[256,256]{0,1:T(8,128)(4,1)} %get-tuple-element.23) | copy-start | bytes 196612
  634.2 16.9 %slice-start.2 = ((s8[8388608]{0:T(1024)(128)(4,1)}), s8[4194304]{0:T(1024)(128)(4,1)S(1)}, s32[]{:S(2)}) async-start(s8[8388608]{0:T(1024)(128)(4,1)} %bitcast.171), calls=%async_computation.6 | async-start | bytes 8388608
  642.7 8.5 %slice-start.3 = ((s8[8388608]{0:T(1024)(128)(4,1)}), s8[4194304]{0:T(1024)(128)(4,1)S(1)}, s32[]{:S(2)}) async-start(s8[8388608]{0:T(1024)(128)(4,1)} %bitcast.171), calls=%async_computation.7 | async-start | bytes 8388608
where the time goes:
time: 681 us; the launch traced here: 672 us
  matrix products  245 us (36%)
  starting transfers between devices  242 us (36%)
  waiting for transfers between devices  126 us (19%)
  local copies, waits for them, and re-layouts  43.5 us (6%)
  other arithmetic  14.4 us (2%)
    ppermute x24, starting transfers between devices, shifted(): lax.ppermute(value, axis, [(source, source + steps) for source in range(l...  221 us
    ppermute x24, waiting for transfers between devices, shifted(): lax.ppermute(value, axis, [(source, source + steps) for source in range(l...  67.7 us
    dot_general x5, matrix products, per_device(): jnp.einsum('hqk,hkd->hqd', dscores, k_blk, preferred_element_type=jnp.flo...  55.1 us
    dot_general x9, matrix products, scores(): jnp.einsum('hqd,hkd->hqk', q_blk, k_blk, preferred_element_type=jnp.float32)  49.5 us
    dot_general x4, matrix products, per_device(): jnp.einsum('hqk,hqd->hkd', dscores, q_blk, preferred_element_type=jnp.flo...  45.8 us
    dot_general x5, matrix products, per_device(): jnp.einsum('hqk,hkd->hqd', probs[index].astype(jnp.bfloat16), value_list[...  40.7 us
    dot_general x4, matrix products, per_device(): jnp.einsum('hqk,hqd->hkd', prob_bf, d_blk, preferred_element_type=jnp.flo...  34.4 us
    unnamed x55, local copies, waits for them, and re-layouts  24 us
  transfers between devices with their start and end apart: 28, of which 7 were waited for; matrix products, arithmetic and copies ran while one was open for 36% of the time, Pallas kernels for 0%

commit v1 on v0

--- a/solution.py
+++ b/solution.py
@@ -19,7 +19,12 @@
     query, keys, values, dout = (
         lax.all_to_all(attn_q, "head", split_axis=1, concat_axis=0, tiled=True),
         lax.all_to_all(attn_k, "head", split_axis=1, concat_axis=0, tiled=True),
-        lax.all_to_all(attn_v, "head", split_axis=1, concat_axis=0, tiled=True),
+        jnp.concatenate(
+            lax.all_to_all(
+                jnp.stack(jnp.split(attn_v, lax.axis_size("head"), axis=1)), "head", 0, 0
+            ),
+            axis=0,
+        ),
         lax.all_to_all(attn_dout, "head", split_axis=1, concat_axis=0, tiled=True),
     )
     tok = query.shape[0]

time: 681 us -> 681 us (level)
  no operation moved by 1% of the time
where the time goes in v1:
time: 681 us; the launch traced here: 672 us
  matrix products  245 us (36%)
  starting transfers between devices  242 us (36%)
  waiting for transfers between devices  125 us (18%)
  local copies, waits for them, and re-layouts  42.1 us (6%)
  other arithmetic  15.9 us (2%)
    ppermute x24, starting transfers between devices, shifted(): lax.ppermute(value, axis, [(source, source + steps) for source in range(l...  221 us
    ppermute x24, waiting for transfers between devices, shifted(): lax.ppermute(value, axis, [(source, source + steps) for source in range(l...  67.7 us
    dot_general x5, matrix products, per_device(): jnp.einsum('hqk,hkd->hqd', dscores, k_blk, preferred_element_type=jnp.flo...  55 us
    dot_general x9, matrix products, scores(): jnp.einsum('hqd,hkd->hqk', q_blk, k_blk, preferred_element_type=jnp.float32)  49.5 us
    dot_general x4, matrix products, per_device(): jnp.einsum('hqk,hqd->hkd', dscores, q_blk, preferred_element_type=jnp.flo...  45.9 us
    dot_general x5, matrix products, per_device(): jnp.einsum('hqk,hkd->hqd', probs[index].astype(jnp.bfloat16), value_list[...  40.7 us
    dot_general x4, matrix products, per_device(): jnp.einsum('hqk,hqd->hkd', prob_bf, d_blk, preferred_element_type=jnp.flo...  34.4 us
    unnamed x55, local copies, waits for them, and re-layouts  24 us
  transfers between devices with their start and end apart: 28, of which 7 were waited for; matrix products, arithmetic and copies ran while one was open for 36% of the time, Pallas kernels for 0%

profile of v1, /device:TPU:31, one launch (start us, length us, event | category | flops | bytes accessed | tf_op | source)
XLA Modules:
  0.0 672.0 jit_solution(7475605377161647644)
XLA Ops:
  0.6 3.1 copy.241
  3.8 4.0 all-to-all-start.1
  7.7 3.1 copy.242
  10.9 20.0 %all-to-all-done.1 = bf16[128,2,4096]{2,0,1:T(8,128)(2,1)S(1)} async-done(((bf16[128,2,4096]{2,0,1:T(8,128)(2,1)}), bf16[128,2,4096]{2,0,1:T(8,128)(2,1)S(1)}, u32[]{:S(2)}, u32[]{:S(2)}) %all-to-all-start.1) | async-done | bytes 2097184 | tf_op jit(solution)/shard_map/all_to_all | solution.py:21
  32.2 4.9 all-to-all-start
  40.2 19.0 %all-to-all-done = bf16[128,2,4096]{2,0,1:T(8,128)(2,1)S(1)} async-done(((bf16[128,2,4096]{2,0,1:T(8,128)(2,1)}), bf16[128,2,4096]{2,0,1:T(8,128)(2,1)S(1)}, u32[]{:S(2)}, u32[]{:S(2)}) %all-to-all-start) | async-done | bytes 2097184 | tf_op jit(solution)/shard_map/all_to_all | solution.py:20
  59.2 6.0 all-to-all-start.2
  65.2 2.2 copy.180
  72.3 14.2 %all-to-all-done.2 = bf16[2,128,4096]{2,1,0:T(8,128)(2,1)} async-done(((bf16[2,128,4096]{2,1,0:T(8,128)(2,1)}), bf16[2,128,4096]{2,1,0:T(8,128)(2,1)}, u32[]{:S(2)}, u32[]{:S(2)}) %all-to-all-start.2) | async-done | bytes 2097184 | tf_op jit(solution)/shard_map/all_to_all | solution.py:23
  86.5 6.0 all-to-all-start.3
  98.0 3.4 copy.179
  108.3 4.6 all-to-all-done.3
  112.9 2.2 copy.182
  115.2 2.2 copy.246
  117.4 2.2 copy.243
  119.5 5.9 fusion.18
  127.0 3.9 fusion.21
  130.9 36.0 %collective-permute-done.3 = bf16[32,256,128]{2,1,0:T(8,128)(2,1)} collective-permute-done((bf16[32,256,128]{2,1,0:T(8,128)(2,1)}, bf16[32,256,128]{2,1,0:T(8,128)(2,1)}, u32[]{:S(2)}, u32[]{:S(2)}) %collective-permute-start.3) | collective-permute-done | bytes 2097184 | tf_op jit(solution)/shard_map/ppermute | solution.py:15
  168.2 3.9 fusion.22
  173.5 5.5 fusion.20
  179.0 82.5 %collective-permute-start.16 = (bf16[32,256,128]{2,1,0:T(8,128)(2,1)}, bf16[32,256,128]{2,1,0:T(8,128)(2,1)}, u32[]{:S(2)}, u32[]{:S(2)}) collective-permute-start(bf16[32,256,128]{2,1,0:T(8,128)(2,1)} %bitcast.183), channel_id=1, source_target_pairs={{6,0},{8,2},{10,4},{12,6},{14,8},{16,10},{18,12},{20,14},{22,16},{... | collective-permute-start | bytes 6291464 | tf_op jit(solution)/shard_map/ppermute | solution.py:15
  261.5 7.2 %fusion.19 = (f32[32,256]{1,0:T(8,128)S(1)}, f32[32,256,256]{1,2,0:T(8,128)}) fusion(pred[256,256]{0,1:T(8,128)(4,1)S(1)} %get-tuple-element.27, bf16[32,256,128]{2,1,0:T(8,128)(2,1)} %collective-permute-done, bf16[256,32,128]{2,1,0:T(8,128)(2,1)S(1)} %bitcast.196), kind=kOutput, calls=%fused_computation.47 | convolution fusion | flops 543154176 | bytes 12681216 | tf_op jit(solution)/shard_map/hqd,hkd->hqk/dot_general | solution.py:57
  268.7 12.7 %exponential_reduce_fusion.3 = (f32[32,256]{1,0:T(8,128)S(1)}, f32[32,256]{1,0:T(8,128)S(1)}, f32[32,256]{1,0:T(8,128)S(1)}, f32[32,256]{1,0:T(8,128)S(1)}, f32[32,256]{1,0:T(8,128)S(1)}) fusion(f32[32,256,256]{1,2,0:T(8,128)} %get-tuple-element.43, f32[32,256]{1,0:T(8,128)S(1)} %maximum_maximum_fusion, pred[256,256]{0,1:T(8,128)(4,1)S(1)} %get-tuple-element.27, ...), kind=kLoop, calls=%fused_computation.30 | loop fusion | flops 41902080 | bytes 42467328 | tf_op jit(solution)/shard_map/reduce_sum | solution.py:71
  281.5 3.0 collective-permute-start.12
  284.6 6.2 fusion.33
  290.8 25.0 %collective-permute-start.18 = (bf16[32,256,128]{2,1,0:T(8,128)(2,1)}, bf16[32,256,128]{2,1,0:T(8,128)(2,1)}, u32[]{:S(2)}, u32[]{:S(2)}) collective-permute-start(bf16[32,256,128]{2,1,0:T(8,128)(2,1)} %bitcast.180), channel_id=1, source_target_pairs={{6,0},{8,2},{10,4},{12,6},{14,8},{16,10},{18,12},{20,14},{22,16},{... | collective-permute-start | bytes 6291464 | tf_op jit(solution)/shard_map/ppermute | solution.py:15
  315.8 4.6 fusion.35
  320.4 37.2 %collective-permute-start.14 = (bf16[32,256,128]{2,1,0:T(8,128)(2,1)}, bf16[32,256,128]{2,1,0:T(8,128)(2,1)}, u32[]{:S(2)}, u32[]{:S(2)}) collective-permute-start(bf16[32,256,128]{2,1,0:T(8,128)(2,1)} %bitcast.180), channel_id=1, source_target_pairs={{4,0},{6,2},{8,4},{10,6},{12,8},{14,10},{16,12},{18,14},{20,16},{2... | collective-permute-start | bytes 6291464 | tf_op jit(solution)/shard_map/ppermute | solution.py:15
  357.6 6.2 fusion.37
  363.8 9.1 %fusion.125 = f32[32,256,128]{2,1,0:T(8,128)} fusion(bf16[32,256,128]{2,0,1:T(8,128)(2,1)S(1)} %bitcast.210, f32[32,256,256]{1,2,0:T(8,128)} %get-tuple-element.41, f32[32,256]{1,0:T(8,128)S(1)} %log_add_fusion, pred[256,256]{0,1:T(8,128)(4,1)S(1)} %get-tuple-element.26), kind=kOutput, calls=%fused_computation.137 | convolution fusion | flops 547356672 | bytes 14778368 | tf_op jit(solution)/shard_map/hqk,hkd->hqd/dot_general | solution.py:80
  372.9 17.5 %collective-permute-done.7 = bf16[32,256,128]{2,1,0:T(8,128)(2,1)} collective-permute-done((bf16[32,256,128]{2,1,0:T(8,128)(2,1)}, bf16[32,256,128]{2,1,0:T(8,128)(2,1)}, u32[]{:S(2)}, u32[]{:S(2)}) %collective-permute-start.7) | collective-permute-done | bytes 2097184 | tf_op jit(solution)/shard_map/ppermute | solution.py:15
  390.4 2.9 collective-permute-start.8
  393.3 14.4 %multiply_reduce_fusion = f32[32,256]{1,0:T(8,128)S(1)} fusion(f32[32,256,128]{2,1,0:T(8,128)} %fusion.33, f32[32,256,128]{2,1,0:T(8,128)} %fusion.35, f32[32,256,128]{2,1,0:T(8,128)} %fusion.125, f32[32,256,128]{2,1,0:T(8,128)} %fusion.37, bf16[32,256,128]{2,1,0:T(8,128)(2,1)} %collective-permute-done.7, f32[32,256,256]{1,2,0:T(8,128)} %copy-done, ...), kind=kOutput, calls=%fused_computation.66 | convolution fusion | flops 554688512 | bytes 29491200 | tf_op jit(solution)/shard_map/hqk,hkd->hqd/dot_general | solution.py:80
  407.8 10.3 %fusion.8 = bf16[32,256,256]{1,2,0:T(8,128)(2,1)} fusion(f32[32,256,256]{1,2,0:T(8,128)} %get-tuple-element.41, f32[32,256]{1,0:T(8,128)S(1)} %multiply_reduce_fusion, f32[32,256]{1,0:T(8,128)S(1)} %log_add_fusion, pred[256,256]{0,1:T(8,128)(4,1)S(1)} %get-tuple-element.26, bf16[256,32,128]{2,1,0:T(8,128)(2,1)} %bitcast.209, bf16[256,32,128]{2,1,0:T(8,128)(2,1)} %bitcast.200), kind=kOutput, calls=%fused_computation.17 | convolution fusion | flops 551550976 | bytes 16908288 | tf_op jit(solution)/shard_map/hqd,hkd->hqk/dot_general | solution.py:99
  418.1 11.7 %fusion.75 = f32[32,256,128]{1,2,0:T(8,128)} fusion(bf16[32,256,128]{2,1,0:T(8,128)(2,1)} %collective-permute-done.2, f32[32,256,256]{1,2,0:T(8,128)} %copy-done.5, f32[32,256]{1,0:T(8,128)S(1)} %multiply_reduce_fusion, f32[32,256]{1,0:T(8,128)S(1)} %log_add_fusion, pred[256,256]{0,1:T(8,128)(4,1)S(1)} %get-tuple-element.29, ...), kind=kOutput, calls=%fused_computation.97 | convolution fusion | flops 1088421888 | bytes 19005440 | tf_op jit(solution)/shard_map/hqk,hkd->hqd/dot_general | solution.py:101
  429.7 11.5 %fusion.73 = f32[32,256,128]{1,2,0:T(8,128)} fusion(bf16[32,256,128]{2,1,0:T(8,128)(2,1)} %collective-permute-done.1, f32[32,256,256]{1,2,0:T(8,128)} %copy-done.6, f32[32,256]{1,0:T(8,128)S(1)} %multiply_reduce_fusion, f32[32,256]{1,0:T(8,128)S(1)} %log_add_fusion, pred[256,256]{0,1:T(8,128)(4,1)S(1)} %get-tuple-element.28, ...), kind=kOutput, calls=%fused_computation.96 | convolution fusion | flops 1088421888 | bytes 19005440 | tf_op jit(solution)/shard_map/hqk,hkd->hqd/dot_general | solution.py:101
  441.2 11.4 %fusion.71 = f32[32,256,128]{1,2,0:T(8,128)} fusion(bf16[32,256,128]{2,1,0:T(8,128)(2,1)} %collective-permute-done, f32[32,256,256]{1,2,0:T(8,128)} %get-tuple-element.43, f32[32,256]{1,0:T(8,128)S(1)} %multiply_reduce_fusion, f32[32,256]{1,0:T(8,128)S(1)} %log_add_fusion, pred[256,256]{0,1:T(8,128)(4,1)S(1)} %get-tuple-element.27, ...), kind=kOutput, calls=%fused_computation.95 | convolution fusion | flops 1088421888 | bytes 19005440 | tf_op jit(solution)/shard_map/hqk,hkd->hqd/dot_general | solution.py:101
  452.7 5.8 fusion.123
  458.4 14.7 %multiply_convert_fusion.1 = bf16[32,256,128]{1,2,0:T(8,128)(2,1)} fusion(f32[32,256,128]{1,2,0:T(8,128)} %fusion.75, f32[32,256,128]{1,2,0:T(8,128)} %fusion.73, f32[32,256,128]{1,2,0:T(8,128)} %fusion.123, f32[32,256,128]{1,2,0:T(8,128)} %fusion.71, bf16[32,256,128]{2,1,0:T(8,128)(2,1)} %collective-permute-done.3, f32[32,256,256]{1,2,0:T(8,128)} %copy-done, ...), kind=kOutput, calls=%fused_computation.60 | convolution fusion | flops 1094713344 | bytes 33685504 | tf_op jit(solution)/shard_map/hqk,hkd->hqd/dot_general | solution.py:101
  474.8 6.1 fusion.190
  480.9 2.6 collective-permute-start.10
  483.5 6.3 fusion.191
  489.8 2.8 collective-permute-start.19
  492.6 6.1 fusion.192
  498.8 5.3 fusion.119
  504.1 14.1 %collective-permute-done.20 = bf16[32,256,128]{2,1,0:T(8,128)(2,1)S(1)} collective-permute-done((bf16[32,256,128]{2,1,0:T(8,128)(2,1)}, bf16[32,256,128]{2,1,0:T(8,128)(2,1)S(1)}, u32[]{:S(2)}, u32[]{:S(2)}) %collective-permute-start.20) | collective-permute-done | bytes 2097184 | tf_op jit(solution)/shard_map/ppermute | solution.py:15
  519.6 4.6 fusion.193
  524.1 3.7 fusion.121
  527.8 4.2 copy.116
  532.0 5.7 collective-permute-start.22
  539.2 2.4 collective-permute-start.13
  541.6 10.9 %fusion.83 = f32[32,256,128]{1,2,0:T(8,128)} fusion(bf16[32,256,128]{2,1,0:T(8,128)(2,1)} %collective-permute-done.16, f32[32,256,256]{1,2,0:T(8,128)} %fusion.190, f32[32,256]{1,0:T(8,128)S(1)} %collective-permute-done.19, f32[32,256]{1,0:T(8,128)S(1)} %collective-permute-done.17, pred[256,256]{0,1:T(8,128)(4,1)S(1)} %get-tuple-element.33, ...), kind=kOutput, calls=%fused_computation.101 | convolution fusion | flops 1088421888 | bytes 19005440 | tf_op jit(solution)/shard_map/hqk,hqd->hkd/dot_general | solution.py:121
  552.5 10.3 %collective-permute-start.11 = (f32[32,256]{1,0:T(8,128)S(1)}, f32[32,256]{1,0:T(8,128)S(1)}, u32[]{:S(2)}, u32[]{:S(2)}) collective-permute-start(f32[32,256]{1,0:T(8,128)S(1)} %multiply_reduce_fusion), channel_id=1, source_target_pairs={{2,0},{4,2},{6,4},{8,6},{10,8},{12,10},{14,12},{16,14},{18,16},{20... | collective-permute-start | bytes 98312 | tf_op jit(solution)/shard_map/ppermute | solution.py:15
  562.8 4.7 collective-permute-start.9
  567.6 25.2 %collective-permute-start.23 = (f32[32,256]{1,0:T(8,128)S(1)}, f32[32,256]{1,0:T(8,128)S(1)}, u32[]{:S(2)}, u32[]{:S(2)}) collective-permute-start(f32[32,256]{1,0:T(8,128)S(1)} %multiply_reduce_fusion), channel_id=1, source_target_pairs={{8,0},{10,2},{12,4},{14,6},{16,8},{18,10},{20,12},{22,14},{24,16},... | collective-permute-start | bytes 98312 | tf_op jit(solution)/shard_map/ppermute | solution.py:15
  592.8 10.9 %fusion.81 = f32[32,256,128]{1,2,0:T(8,128)} fusion(bf16[32,256,128]{2,1,0:T(8,128)(2,1)} %collective-permute-done.12, f32[32,256,256]{1,2,0:T(8,128)} %fusion.191, f32[32,256]{1,0:T(8,128)S(1)} %collective-permute-done.15, f32[32,256]{1,0:T(8,128)S(1)} %collective-permute-done.13, pred[256,256]{0,1:T(8,128)(4,1)S(1)} %get-tuple-element.32, ...), kind=kOutput, calls=%fused_computation.100 | convolution fusion | flops 1088421888 | bytes 19005440 | tf_op jit(solution)/shard_map/hqk,hqd->hkd/dot_general | solution.py:121
  605.9 11.0 %fusion.79 = f32[32,256,128]{1,2,0:T(8,128)} fusion(bf16[32,256,128]{2,1,0:T(8,128)(2,1)} %collective-permute-done.8, f32[32,256,256]{1,2,0:T(8,128)} %fusion.192, f32[32,256]{1,0:T(8,128)S(1)} %collective-permute-done.11, f32[32,256]{1,0:T(8,128)S(1)} %collective-permute-done.9, pred[256,256]{0,1:T(8,128)(4,1)S(1)} %get-tuple-element.31, ...), kind=kOutput, calls=%fused_computation.99 | convolution fusion | flops 1088421888 | bytes 19005440 | tf_op jit(solution)/shard_map/hqk,hqd->hkd/dot_general | solution.py:121
  616.9 13.1 %multiply_convert_fusion = bf16[32,256,128]{1,2,0:T(8,128)(2,1)} fusion(f32[32,256,128]{1,2,0:T(8,128)} %fusion.83, f32[32,256,128]{1,2,0:T(8,128)} %fusion.81, f32[32,256,128]{1,2,0:T(8,128)} %fusion.121, f32[32,256,128]{1,2,0:T(8,128)} %fusion.79, bf16[32,256,128]{2,1,0:T(8,128)(2,1)} %copy-done.12, f32[32,256,256]{1,2,0:T(8,128)} %fusion.193, ...), kind=kOutput, calls=%fused_computation.59 | convolution fusion | flops 1094713344 | bytes 33685504 | tf_op jit(solution)/shard_map/hqk,hqd->hkd/dot_general | solution.py:121
  630.0 4.3 copy.117
  634.3 8.4 %fusion.25 = f32[32,256,128]{1,2,0:T(8,128)} fusion(bf16[32,256,128]{2,1,0:T(8,128)(2,1)} %collective-permute-done.18, f32[32,256,256]{1,2,0:T(8,128)} %fusion.190, f32[32,256]{1,0:T(8,128)S(1)} %collective-permute-done.17, pred[256,256]{0,1:T(8,128)(4,1)S(1)} %get-tuple-element.33), kind=kOutput, calls=%fused_computation.52 | convolution fusion | flops 547356672 | bytes 14778368 | tf_op jit(solution)/shard_map/hqk,hqd->hkd/dot_general | solution.py:123
  642.7 8.5 %fusion.27 = f32[32,256,128]{1,2,0:T(8,128)} fusion(bf16[32,256,128]{2,1,0:T(8,128)(2,1)} %collective-permute-done.14, f32[32,256,256]{1,2,0:T(8,128)} %fusion.191, f32[32,256]{1,0:T(8,128)S(1)} %collective-permute-done.13, pred[256,256]{0,1:T(8,128)(4,1)S(1)} %get-tuple-element.32), kind=kOutput, calls=%fused_computation.53 | convolution fusion | flops 547356672 | bytes 14778368 | tf_op jit(solution)/shard_map/hqk,hqd->hkd/dot_general | solution.py:123
  651.2 5.9 fusion.29
  657.2 11.5 %add_convert_fusion = bf16[32,256,128]{1,2,0:T(8,128)(2,1)S(1)} fusion(f32[32,256,128]{1,2,0:T(8,128)} %fusion.25, f32[32,256,128]{1,2,0:T(8,128)} %fusion.27, f32[32,256,128]{1,2,0:T(8,128)} %fusion.119, f32[32,256,128]{1,2,0:T(8,128)} %fusion.29, bf16[32,256,128]{2,1,0:T(8,128)(2,1)} %collective-permute-done.22, f32[32,256,256]{1,2,0:T(8,128)} %fusion.193, ...), kind=kOutput, calls=%fused_computation.61 | convolution fusion | flops 552599552 | bytes 29458432 | tf_op jit(solution)/shard_map/hqk,hqd->hkd/dot_general | solution.py:123
  668.7 2.9 copy.118
  (99 shorter events, 32.5 us)
Async XLA Ops:
  3.8 27.1 %all-to-all-start.1 = ((bf16[128,2,4096]{2,0,1:T(8,128)(2,1)}), bf16[128,2,4096]{2,0,1:T(8,128)(2,1)S(1)}, u32[]{:S(2)}, u32[]{:S(2)}) async-start(bf16[128,2,4096]{2,0,1:T(8,128)(2,1)} %bitcast.224), calls=%async_computation.1 | async-start | bytes 4194304 | tf_op jit(solution)/shard_map/all_to_all | solution.py:21
  30.8 1.3 copy-start.13
  32.2 27.0 %all-to-all-start = ((bf16[128,2,4096]{2,0,1:T(8,128)(2,1)}), bf16[128,2,4096]{2,0,1:T(8,128)(2,1)S(1)}, u32[]{:S(2)}, u32[]{:S(2)}) async-start(bf16[128,2,4096]{2,0,1:T(8,128)(2,1)} %bitcast.223), calls=%async_computation | async-start | bytes 4194304 | tf_op jit(solution)/shard_map/all_to_all | solution.py:20
  59.2 6.0 copy-start.11
  59.2 27.3 %all-to-all-start.2 = ((bf16[2,128,4096]{2,1,0:T(8,128)(2,1)}), bf16[2,128,4096]{2,1,0:T(8,128)(2,1)}, u32[]{:S(2)}, u32[]{:S(2)}) async-start(bf16[2,128,4096]{2,1,0:T(8,128)(2,1)} %pad_maximum_fusion), calls=%async_computation.2 | async-start | bytes 4194304 | tf_op jit(solution)/shard_map/all_to_all | solution.py:23
  65.2 5.6 copy-start.14
  69.5 55.9 %collective-permute-start.2 = (bf16[32,256,128]{2,1,0:T(8,128)(2,1)}, bf16[32,256,128]{2,1,0:T(8,128)(2,1)}, u32[]{:S(2)}, u32[]{:S(2)}) collective-permute-start(bf16[32,256,128]{2,1,0:T(8,128)(2,1)} %bitcast.182), channel_id=1, source_target_pairs={{0,6},{2,8},{4,10},{6,12},{8,14},{10,16},{12,18},{14,20},{16,22},{... | collective-permute-start | bytes 6291464 | tf_op jit(solution)/shard_map/ppermute | solution.py:15
  70.8 23.0 %copy-start.16 = (s32[4096]{0:T(1024)S(1)}, s32[4096]{0:T(1024)}, u32[]{:S(2)}) copy-start(s32[4096]{0:T(1024)} %param.9) | copy-start | bytes 49156
  86.5 26.4 %all-to-all-start.3 = ((bf16[128,2,4096]{2,0,1:T(8,128)(2,1)}), bf16[128,2,4096]{2,0,1:T(8,128)(2,1)}, u32[]{:S(2)}, u32[]{:S(2)}) async-start(bf16[128,2,4096]{2,0,1:T(8,128)(2,1)} %bitcast.221), calls=%async_computation.3 | async-start | bytes 4194304 | tf_op jit(solution)/shard_map/all_to_all | solution.py:28
  92.5 74.5 %collective-permute-start.3 = (bf16[32,256,128]{2,1,0:T(8,128)(2,1)}, bf16[32,256,128]{2,1,0:T(8,128)(2,1)}, u32[]{:S(2)}, u32[]{:S(2)}) collective-permute-start(bf16[32,256,128]{2,1,0:T(8,128)(2,1)} %bitcast.182), channel_id=1, source_target_pairs={{0,8},{2,10},{4,12},{6,14},{8,16},{10,18},{12,20},{14,22},{16,24},... | collective-permute-start | bytes 6291464 | tf_op jit(solution)/shard_map/ppermute | solution.py:15
  94.0 78.2 %collective-permute-start.1 = (bf16[32,256,128]{2,1,0:T(8,128)(2,1)}, bf16[32,256,128]{2,1,0:T(8,128)(2,1)}, u32[]{:S(2)}, u32[]{:S(2)}) collective-permute-start(bf16[32,256,128]{2,1,0:T(8,128)(2,1)} %bitcast.182), channel_id=1, source_target_pairs={{0,4},{2,6},{4,8},{6,10},{8,12},{10,14},{12,16},{14,18},{16,20},{1... | collective-permute-start | bytes 6291464 | tf_op jit(solution)/shard_map/ppermute | solution.py:15
  96.7 82.3 %collective-permute-start = (bf16[32,256,128]{2,1,0:T(8,128)(2,1)}, bf16[32,256,128]{2,1,0:T(8,128)(2,1)}, u32[]{:S(2)}, u32[]{:S(2)}) collective-permute-start(bf16[32,256,128]{2,1,0:T(8,128)(2,1)} %bitcast.182), channel_id=1, source_target_pairs={{0,2},{2,4},{4,6},{6,8},{8,10},{10,12},{12,14},{14,16},{16,18},{18... | collective-permute-start | bytes 6291464 | tf_op jit(solution)/shard_map/ppermute | solution.py:15
  103.5 1.4 copy-start.7
  107.0 174.5 %collective-permute-start.6 = (bf16[32,256,128]{2,1,0:T(8,128)(2,1)}, bf16[32,256,128]{2,1,0:T(8,128)(2,1)}, u32[]{:S(2)}, u32[]{:S(2)}) collective-permute-start(bf16[32,256,128]{2,1,0:T(8,128)(2,1)} %bitcast.181), channel_id=1, source_target_pairs={{0,6},{2,8},{4,10},{6,12},{8,14},{10,16},{12,18},{14,20},{16,22},{... | collective-permute-start | bytes 6291464 | tf_op jit(solution)/shard_map/ppermute | solution.py:15
  112.9 2.2 copy-start.1
  115.1 4.4 copy-start.3
  125.5 165.3 %collective-permute-start.5 = (bf16[32,256,128]{2,1,0:T(8,128)(2,1)}, bf16[32,256,128]{2,1,0:T(8,128)(2,1)S(1)}, u32[]{:S(2)}, u32[]{:S(2)}) collective-permute-start(bf16[32,256,128]{2,1,0:T(8,128)(2,1)} %bitcast.181), channel_id=1, source_target_pairs={{0,4},{2,6},{4,8},{6,10},{8,12},{10,14},{12,16},{14,18},{16,20},{1... | collective-permute-start | bytes 6291464 | tf_op jit(solution)/shard_map/ppermute | solution.py:15
  130.9 153.6 %copy-start.5 = (f32[32,256,256]{1,2,0:T(8,128)}, f32[32,256,256]{1,2,0:T(8,128)S(1)}, u32[]{:S(2)}) copy-start(f32[32,256,256]{1,2,0:T(8,128)S(1)} %get-tuple-element.37) | copy-start | bytes 25165828
  167.0 153.5 %collective-permute-start.4 = (bf16[32,256,128]{2,1,0:T(8,128)(2,1)}, bf16[32,256,128]{2,1,0:T(8,128)(2,1)}, u32[]{:S(2)}, u32[]{:S(2)}) collective-permute-start(bf16[32,256,128]{2,1,0:T(8,128)(2,1)} %bitcast.181), channel_id=1, source_target_pairs={{0,2},{2,4},{4,6},{6,8},{8,10},{10,12},{12,14},{14,16},{16,18},{18... | collective-permute-start | bytes 6291464 | tf_op jit(solution)/shard_map/ppermute | solution.py:15
  172.2 96.6 %copy-start = (f32[32,256,256]{1,2,0:T(8,128)}, f32[32,256,256]{1,2,0:T(8,128)S(1)}, u32[]{:S(2)}) copy-start(f32[32,256,256]{1,2,0:T(8,128)S(1)} %get-tuple-element.35) | copy-start | bytes 25165828
  172.2 218.2 %collective-permute-start.7 = (bf16[32,256,128]{2,1,0:T(8,128)(2,1)}, bf16[32,256,128]{2,1,0:T(8,128)(2,1)}, u32[]{:S(2)}, u32[]{:S(2)}) collective-permute-start(bf16[32,256,128]{2,1,0:T(8,128)(2,1)} %bitcast.181), channel_id=1, source_target_pairs={{0,8},{2,10},{4,12},{6,14},{8,16},{10,18},{12,20},{14,22},{16,24},... | collective-permute-start | bytes 6291464 | tf_op jit(solution)/shard_map/ppermute | solution.py:15
  179.0 136.8 %copy-start.6 = (f32[32,256,256]{1,2,0:T(8,128)}, f32[32,256,256]{1,2,0:T(8,128)S(1)}, u32[]{:S(2)}) copy-start(f32[32,256,256]{1,2,0:T(8,128)S(1)} %get-tuple-element.39) | copy-start | bytes 25165828
  179.0 294.1 %collective-permute-start.16 = (bf16[32,256,128]{2,1,0:T(8,128)(2,1)}, bf16[32,256,128]{2,1,0:T(8,128)(2,1)}, u32[]{:S(2)}, u32[]{:S(2)}) collective-permute-start(bf16[32,256,128]{2,1,0:T(8,128)(2,1)} %bitcast.183), channel_id=1, source_target_pairs={{6,0},{8,2},{10,4},{12,6},{14,8},{16,10},{18,12},{20,14},{22,16},{... | collective-permute-start | bytes 6291464 | tf_op jit(solution)/shard_map/ppermute | solution.py:15
  281.5 199.5 %collective-permute-start.12 = (bf16[32,256,128]{2,1,0:T(8,128)(2,1)}, bf16[32,256,128]{2,1,0:T(8,128)(2,1)}, u32[]{:S(2)}, u32[]{:S(2)}) collective-permute-start(bf16[32,256,128]{2,1,0:T(8,128)(2,1)} %bitcast.183), channel_id=1, source_target_pairs={{4,0},{6,2},{8,4},{10,6},{12,8},{14,10},{16,12},{18,14},{20,16},{2... | collective-permute-start | bytes 6291464 | tf_op jit(solution)/shard_map/ppermute | solution.py:15
  290.8 29.6 %copy-start.17 = (bf16[32,256,128]{2,1,0:T(8,128)(2,1)}, bf16[32,256,128]{2,1,0:T(8,128)(2,1)S(1)}, u32[]{:S(2)}) copy-start(bf16[32,256,128]{2,1,0:T(8,128)(2,1)S(1)} %collective-permute-done.5) | copy-start | bytes 6291460
  290.8 66.8 %slice-start = ((s8[8388608]{0:T(1024)(128)(4,1)}), s8[4194304]{0:T(1024)(128)(4,1)S(1)}, s32[]{:S(2)}) async-start(s8[8388608]{0:T(1024)(128)(4,1)} %bitcast.206), calls=%async_computation.4 | async-start | bytes 8388608
  290.8 66.8 %slice-start.1 = ((s8[8388608]{0:T(1024)(128)(4,1)}), s8[4194304]{0:T(1024)(128)(4,1)S(1)}, s32[]{:S(2)}) async-start(s8[8388608]{0:T(1024)(128)(4,1)} %bitcast.206), calls=%async_computation.5 | async-start | bytes 8388608
  290.8 241.2 %collective-permute-start.18 = (bf16[32,256,128]{2,1,0:T(8,128)(2,1)}, bf16[32,256,128]{2,1,0:T(8,128)(2,1)}, u32[]{:S(2)}, u32[]{:S(2)}) collective-permute-start(bf16[32,256,128]{2,1,0:T(8,128)(2,1)} %bitcast.180), channel_id=1, source_target_pairs={{6,0},{8,2},{10,4},{12,6},{14,8},{16,10},{18,12},{20,14},{22,16},{... | collective-permute-start | bytes 6291464 | tf_op jit(solution)/shard_map/ppermute | solution.py:15
  320.4 43.4 %copy-start.8 = (bf16[32,8,32,128]{3,2,1,0:T(8,128)(2,1)S(1)}, bf16[32,8,32,128]{3,2,1,0:T(8,128)(2,1)}, u32[]{:S(2)}) copy-start(bf16[32,8,32,128]{3,2,1,0:T(8,128)(2,1)} %copy-done.7) | copy-start | bytes 6291460
  320.4 232.1 %collective-permute-start.14 = (bf16[32,256,128]{2,1,0:T(8,128)(2,1)}, bf16[32,256,128]{2,1,0:T(8,128)(2,1)}, u32[]{:S(2)}, u32[]{:S(2)}) collective-permute-start(bf16[32,256,128]{2,1,0:T(8,128)(2,1)} %bitcast.180), channel_id=1, source_target_pairs={{4,0},{6,2},{8,4},{10,6},{12,8},{14,10},{16,12},{18,14},{20,16},{2... | collective-permute-start | bytes 6291464 | tf_op jit(solution)/shard_map/ppermute | solution.py:15
  390.4 99.4 %collective-permute-start.8 = (bf16[32,256,128]{2,1,0:T(8,128)(2,1)}, bf16[32,256,128]{2,1,0:T(8,128)(2,1)}, u32[]{:S(2)}, u32[]{:S(2)}) collective-permute-start(bf16[32,256,128]{2,1,0:T(8,128)(2,1)} %bitcast.183), channel_id=1, source_target_pairs={{2,0},{4,2},{6,4},{8,6},{10,8},{12,10},{14,12},{16,14},{18,16},{20... | collective-permute-start | bytes 6291464 | tf_op jit(solution)/shard_map/ppermute | solution.py:15
  473.1 45.2 %collective-permute-start.20 = (bf16[32,256,128]{2,1,0:T(8,128)(2,1)}, bf16[32,256,128]{2,1,0:T(8,128)(2,1)S(1)}, u32[]{:S(2)}, u32[]{:S(2)}) collective-permute-start(bf16[32,256,128]{2,1,0:T(8,128)(2,1)} %bitcast.183), channel_id=1, source_target_pairs={{8,0},{10,2},{12,4},{14,6},{16,8},{18,10},{20,12},{22,14},{24,16},... | collective-permute-start | bytes 6291464 | tf_op jit(solution)/shard_map/ppermute | solution.py:15
  480.9 122.8 %collective-permute-start.10 = (bf16[32,256,128]{2,1,0:T(8,128)(2,1)}, bf16[32,256,128]{2,1,0:T(8,128)(2,1)}, u32[]{:S(2)}, u32[]{:S(2)}) collective-permute-start(bf16[32,256,128]{2,1,0:T(8,128)(2,1)} %bitcast.180), channel_id=1, source_target_pairs={{2,0},{4,2},{6,4},{8,6},{10,8},{12,10},{14,12},{16,14},{18,16},{20... | collective-permute-start | bytes 6291464 | tf_op jit(solution)/shard_map/ppermute | solution.py:15
  483.5 15.3 %slice-start.4 = ((s8[8388608]{0:T(1024)(128)(4,1)}), s8[4194304]{0:T(1024)(128)(4,1)S(1)}, s32[]{:S(2)}) async-start(s8[8388608]{0:T(1024)(128)(4,1)} %bitcast.225), calls=%async_computation.8 | async-start | bytes 8388608
  489.8 9.0 %copy-start.4 = (bf16[32,8,32,128]{3,2,1,0:T(8,128)(2,1)S(1)}, bf16[32,8,32,128]{3,2,1,0:T(8,128)(2,1)}, u32[]{:S(2)}) copy-start(bf16[32,8,32,128]{3,2,1,0:T(8,128)(2,1)} %copy-done.3) | copy-start | bytes 6291460
  489.8 9.0 %slice-start.5 = ((s8[8388608]{0:T(1024)(128)(4,1)}), s8[4194304]{0:T(1024)(128)(4,1)S(1)}, s32[]{:S(2)}) async-start(s8[8388608]{0:T(1024)(128)(4,1)} %bitcast.225), calls=%async_computation.9 | async-start | bytes 8388608
  489.8 47.9 %collective-permute-start.19 = (f32[32,256]{1,0:T(8,128)S(1)}, f32[32,256]{1,0:T(8,128)S(1)}, u32[]{:S(2)}, u32[]{:S(2)}) collective-permute-start(f32[32,256]{1,0:T(8,128)S(1)} %multiply_reduce_fusion), channel_id=1, source_target_pairs={{6,0},{8,2},{10,4},{12,6},{14,8},{16,10},{18,12},{20,14},{22,16},{... | collective-permute-start | bytes 98312 | tf_op jit(solution)/shard_map/ppermute | solution.py:15
  504.1 20.0 %copy-start.2 = (bf16[32,8,32,128]{3,2,1,0:T(8,128)(2,1)S(1)}, bf16[32,8,32,128]{3,2,1,0:T(8,128)(2,1)}, u32[]{:S(2)}) copy-start(bf16[32,8,32,128]{3,2,1,0:T(8,128)(2,1)} %copy.179) | copy-start | bytes 6291460
  504.1 20.0 %copy-start.10 = (bf16[32,256,256]{1,2,0:T(8,128)(2,1)S(1)}, bf16[32,256,256]{1,2,0:T(8,128)(2,1)}, u32[]{:S(2)}) copy-start(bf16[32,256,256]{1,2,0:T(8,128)(2,1)} %fusion.8) | copy-start | bytes 12582916
  518.3 5.8 copy-start.12
  518.3 20.9 %collective-permute-start.17 = (f32[32,256]{1,0:T(8,128)S(1)}, f32[32,256]{1,0:T(8,128)S(1)}, u32[]{:S(2)}, u32[]{:S(2)}) collective-permute-start(f32[32,256]{1,0:T(8,128)S(1)} %log_add_fusion), channel_id=1, source_target_pairs={{6,0},{8,2},{10,4},{12,6},{14,8},{16,10},{18,12},{20,14},{22,16},{... | collective-permute-start | bytes 98312 | tf_op jit(solution)/shard_map/ppermute | solution.py:15
  527.8 13.8 %copy-start.9 = (bf16[32,8,32,128]{3,2,1,0:T(8,128)(2,1)S(1)}, bf16[32,8,32,128]{3,2,1,0:T(8,128)(2,1)}, u32[]{:S(2)}) copy-start(bf16[32,8,32,128]{3,2,1,0:T(8,128)(2,1)} %copy-done.7) | copy-start | bytes 6291460
  532.0 84.9 %collective-permute-start.22 = (bf16[32,256,128]{2,1,0:T(8,128)(2,1)}, bf16[32,256,128]{2,1,0:T(8,128)(2,1)}, u32[]{:S(2)}, u32[]{:S(2)}) collective-permute-start(bf16[32,256,128]{2,1,0:T(8,128)(2,1)} %bitcast.180), channel_id=1, source_target_pairs={{8,0},{10,2},{12,4},{14,6},{16,8},{18,10},{20,12},{22,14},{24,16},... | collective-permute-start | bytes 6291464 | tf_op jit(solution)/shard_map/ppermute | solution.py:15
  537.7 25.1 %collective-permute-start.15 = (f32[32,256]{1,0:T(8,128)S(1)}, f32[32,256]{1,0:T(8,128)S(1)}, u32[]{:S(2)}, u32[]{:S(2)}) collective-permute-start(f32[32,256]{1,0:T(8,128)S(1)} %multiply_reduce_fusion), channel_id=1, source_target_pairs={{4,0},{6,2},{8,4},{10,6},{12,8},{14,10},{16,12},{18,14},{20,16},{2... | collective-permute-start | bytes 98312 | tf_op jit(solution)/shard_map/ppermute | solution.py:15
  539.2 28.3 %collective-permute-start.13 = (f32[32,256]{1,0:T(8,128)S(1)}, f32[32,256]{1,0:T(8,128)S(1)}, u32[]{:S(2)}, u32[]{:S(2)}) collective-permute-start(f32[32,256]{1,0:T(8,128)S(1)} %log_add_fusion), channel_id=1, source_target_pairs={{4,0},{6,2},{8,4},{10,6},{12,8},{14,10},{16,12},{18,14},{20,16},{2... | collective-permute-start | bytes 98312 | tf_op jit(solution)/shard_map/ppermute | solution.py:15
  552.5 53.4 %collective-permute-start.11 = (f32[32,256]{1,0:T(8,128)S(1)}, f32[32,256]{1,0:T(8,128)S(1)}, u32[]{:S(2)}, u32[]{:S(2)}) collective-permute-start(f32[32,256]{1,0:T(8,128)S(1)} %multiply_reduce_fusion), channel_id=1, source_target_pairs={{2,0},{4,2},{6,4},{8,6},{10,8},{12,10},{14,12},{16,14},{18,16},{20... | collective-permute-start | bytes 98312 | tf_op jit(solution)/shard_map/ppermute | solution.py:15
  562.8 43.0 %collective-permute-start.9 = (f32[32,256]{1,0:T(8,128)S(1)}, f32[32,256]{1,0:T(8,128)S(1)}, u32[]{:S(2)}, u32[]{:S(2)}) collective-permute-start(f32[32,256]{1,0:T(8,128)S(1)} %log_add_fusion), channel_id=1, source_target_pairs={{2,0},{4,2},{6,4},{8,6},{10,8},{12,10},{14,12},{16,14},{18,16},{20... | collective-permute-start | bytes 98312 | tf_op jit(solution)/shard_map/ppermute | solution.py:15
  567.6 49.3 %collective-permute-start.23 = (f32[32,256]{1,0:T(8,128)S(1)}, f32[32,256]{1,0:T(8,128)S(1)}, u32[]{:S(2)}, u32[]{:S(2)}) collective-permute-start(f32[32,256]{1,0:T(8,128)S(1)} %multiply_reduce_fusion), channel_id=1, source_target_pairs={{8,0},{10,2},{12,4},{14,6},{16,8},{18,10},{20,12},{22,14},{24,16},... | collective-permute-start | bytes 98312 | tf_op jit(solution)/shard_map/ppermute | solution.py:15
  603.7 13.2 %collective-permute-start.21 = (f32[32,256]{1,0:T(8,128)S(1)}, f32[32,256]{1,0:T(8,128)S(1)}, u32[]{:S(2)}, u32[]{:S(2)}) collective-permute-start(f32[32,256]{1,0:T(8,128)S(1)} %log_add_fusion), channel_id=1, source_target_pairs={{8,0},{10,2},{12,4},{14,6},{16,8},{18,10},{20,12},{22,14},{24,16},... | collective-permute-start | bytes 98312 | tf_op jit(solution)/shard_map/ppermute | solution.py:15
  605.9 11.0 %copy-start.15 = (pred[256,256]{0,1:T(8,128)(4,1)S(1)}, pred[256,256]{0,1:T(8,128)(4,1)}, u32[]{:S(2)}) copy-start(pred[256,256]{0,1:T(8,128)(4,1)} %get-tuple-element.25) | copy-start | bytes 196612
  634.3 16.9 %slice-start.2 = ((s8[8388608]{0:T(1024)(128)(4,1)}), s8[4194304]{0:T(1024)(128)(4,1)S(1)}, s32[]{:S(2)}) async-start(s8[8388608]{0:T(1024)(128)(4,1)} %bitcast.218), calls=%async_computation.6 | async-start | bytes 8388608
  642.7 8.5 %slice-start.3 = ((s8[8388608]{0:T(1024)(128)(4,1)}), s8[4194304]{0:T(1024)(128)(4,1)S(1)}, s32[]{:S(2)}) async-start(s8[8388608]{0:T(1024)(128)(4,1)} %bitcast.218), calls=%async_computation.7 | async-start | bytes 8388608
